TPU v7x, 32 devices: a whole 2x2x4 slice. The times are simulated.
32 devices in a mesh: panel: 2 (over y), lat: 4 (over z), lon: 4 (over x, core).
Axes of the slice: x: 2, y: 2, z: 4, core: 2. Of those that a mesh axis runs over, the one named last changes fastest.
Arguments:
- state: float32 [2, 7, 2, 256, 512], P('panel', None, None, 'lat', 'lon'), may hold values from -4 to 4
- source_slot: int32 [2, 4, 4, 768], P('panel', 'lat', 'lon'), may hold values from 0 to 3071, as said below
- donor_cell: int32 [2, 4, 4, 192], P('panel', 'lat', 'lon'), may hold values from 0 to 8000
- donor_frac: float32 [2, 4, 4, 2, 192], P('panel', 'lat', 'lon'), may hold values from 0 to 1
- donor_turn: float32 [2, 4, 4, 192], P('panel', 'lat', 'lon'), may hold values from -3.140625 to 3.140625
Outputs:
- new_state: float32 [2, 7, 2, 256, 512], P('panel', None, None, 'lat', 'lon')
Inputs may be any that keep to these rules, and one draw needn't show every extreme that they name: `source_slot`: entries name a partner panel donation (a * 4 + b) * 192 + s. For a device on an edge of its panel, the rim entries that lie on that edge name the donations that fill them; over a panel's whole border every donation of the partner panel is named exactly once. Other entries are unused.
All inputs are finite; a program needn't handle non-finite values.
Results may differ from a plain program's by a relative error of at most 0.00002.
Values sent between devices are 32-bit elements; how exact they have to be, the bound alone decides.
No kernel may reach another device: no remote copies, remote signals or barrier semaphores. Data moves between devices by JAX's collectives and lax.ppermute only.
A program may use at most 64 MiB of HBM per device.

v0:
```python
import jax
import jax.numpy as jnp
from jax import lax
from jax.sharding import PartitionSpec as P

viscosity = 0.05
resistivity = 0.05
diffusivity = 0.05
buoyancy = 0.5
time_step = 0.25
HIGHEST = lax.Precision.HIGHEST


def partner_2(block, axis, apart):
    count = lax.axis_size(axis)
    route = []
    for low in range(count):
        high = low | 1 << apart
        if high != low and high < count:
            route += [(low, high), (high, low)]
    return lax.ppermute(block, axis, route)


def shift(value, axis, step):
    size = lax.axis_size(axis)
    if step > 0:
        route = [(i, i + 1) for i in range(size - 1)]
    else:
        route = [(i + 1, i) for i in range(size - 1)]
    return lax.ppermute(value, axis, route)


def rate(up, mid, down, left, right):
    vert = jnp.concatenate([up, mid, down], axis=2)
    horz = jnp.concatenate([left, mid, right], axis=3)
    height = mid.shape[2]
    width = mid.shape[3]

    def lat_at(k):
        return vert[:, :, 2 + k : 2 + k + height, :]

    def lon_at(k):
        return horz[:, :, :, 2 + k : 2 + k + width]

    middle = mid
    d_lat = (8.0 * (lat_at(1) - lat_at(-1)) - (lat_at(2) - lat_at(-2))) / 12.0
    d_lon = (8.0 * (lon_at(1) - lon_at(-1)) - (lon_at(2) - lon_at(-2))) / 12.0
    padded = jnp.pad(middle, ((0, 0), (1, 1), (0, 0), (0, 0)))
    lap = lat_at(1) + lat_at(-1) + lon_at(1) + lon_at(-1) - 4.0 * middle
    lap = lap + padded[:, 2:] + padded[:, :-2] - 2.0 * middle
    adv_u = middle[1:2] * d_lat + middle[2:3] * d_lon
    adv_b = middle[4:5] * d_lat + middle[5:6] * d_lon
    moment = -adv_u[0:3] + adv_b[3:6] + viscosity * lap[0:3]
    induct = adv_b[0:3] - adv_u[3:6] + resistivity * lap[3:6]
    heat = -adv_u[6:7] + diffusivity * lap[6:7]
    first = moment[0:1] + buoyancy * middle[6:7]
    return jnp.concatenate([first, moment[1:3], induct, heat], axis=0)


def rotate(values, turn):
    cosine = jnp.cos(turn)
    sine = jnp.sin(turn)
    parts = [
        values[0],
        cosine * values[1] - sine * values[2],
        sine * values[1] + cosine * values[2],
        values[3],
        cosine * values[4] - sine * values[5],
        sine * values[4] + cosine * values[5],
        values[6],
    ]
    return jnp.stack(parts)


def per_device(state, source_slot, donor_cell, donor_frac, donor_turn):
    comps = state.shape[1]
    levels = state.shape[2]
    rows = state.shape[3]
    cols = state.shape[4]
    cells = donor_cell[0, 0, 0]
    frac_t = donor_frac[0, 0, 0, 0]
    frac_p = donor_frac[0, 0, 0, 1]
    turn = donor_turn[0, 0, 0]
    slots = source_slot[0, 0, 0]
    lat_pos = lax.axis_index("lat")
    lon_pos = lax.axis_index("lon")
    lat_count = lax.axis_size("lat")
    lon_count = lax.axis_size("lon")
    on_top = lat_pos == 0
    on_bottom = lat_pos == lat_count - 1
    on_left = lon_pos == 0
    on_right = lon_pos == lon_count - 1
    row = cells // (cols - 1)
    col = cells % (cols - 1)
    col_ids = jnp.arange(cols, dtype=jnp.int32)[None, :]
    row_ids = jnp.arange(rows, dtype=jnp.int32)[None, :]
    weight_lon = jnp.where(col_ids == col[:, None], (1.0 - frac_p)[:, None], 0.0) + jnp.where(
        col_ids == col[:, None] + 1, frac_p[:, None], 0.0
    )
    weight_lat = jnp.where(row_ids == row[:, None], (1.0 - frac_t)[:, None], 0.0) + jnp.where(
        row_ids == row[:, None] + 1, frac_t[:, None], 0.0
    )
    band = 2 * cols
    side = 2 * rows
    lat_slots = jnp.where(on_top, slots[0:band], slots[band : 2 * band])
    lon_slots = jnp.where(on_left, slots[2 * band : 2 * band + side], slots[2 * band + side :])
    wanted = jnp.concatenate([lat_slots, lon_slots])
    total = lax.axis_size("lat") * lax.axis_size("lon") * cells.shape[0]
    pick = (jnp.arange(total, dtype=jnp.int32)[:, None] == wanted[None, :]).astype(jnp.float32)

    def donate(field):
        flat = field.reshape(comps * levels, rows, cols)
        along = jnp.einsum("kij,sj->kis", flat, weight_lon, precision=HIGHEST)
        value = jnp.sum(along * weight_lat.T[None], axis=1)
        return rotate(value.reshape(comps, levels, -1), turn).reshape(comps * levels, -1)

    def receive(given):
        whole = lax.all_gather(given, ("lat", "lon"), axis=1, tiled=True)
        partner = partner_2(whole, "panel", 0)
        return jnp.dot(partner, pick, precision=HIGHEST)

    def section(field):
        up = shift(field[:, :, rows - 2 :, :], "lat", 1)
        down = shift(field[:, :, :2, :], "lat", -1)
        left = shift(field[:, :, :, cols - 2 :], "lon", 1)
        right = shift(field[:, :, :, :2], "lon", -1)
        rim = receive(donate(field)).reshape(comps, levels, -1)
        rim_lat = rim[:, :, :band].reshape(comps, levels, 2, cols)
        rim_lon = jnp.transpose(rim[:, :, band:].reshape(comps, levels, 2, rows), (0, 1, 3, 2))
        up = jnp.where(on_top, rim_lat, up)
        down = jnp.where(on_bottom, rim_lat, down)
        left = jnp.where(on_left, rim_lon, left)
        right = jnp.where(on_right, rim_lon, right)
        return rate(up, field, down, left, right)

    field = state[0]
    section_one = field + time_step * section(field)
    second = section(section_one)
    new_field = 0.5 * field + 0.5 * (section_one + time_step * second)
    return new_field[None]


def solution(mesh):
    in_specs = (
        P("panel", None, None, "lat", "lon"),
        P("panel", "lat", "lon", None),
        P("panel", "lat", "lon", None),
        P("panel", "lat", "lon", None, None),
        P("panel", "lat", "lon", None),
    )
    out_specs = P("panel", None, None, "lat", "lon")
    return jax.shard_map(
        per_device, mesh=mesh, in_specs=in_specs, out_specs=out_specs, check_vma=False
    )
```

profile of v0, /device:TPU:1, one launch (start us, length us, event | category | flops | bytes accessed | tf_op | source)
XLA Modules:
  0.0 83.6 jit_solution(6090372736300227283)
XLA Ops:
  0.0 0.7 broadcast_remainder_fusion
  0.7 0.7 compare_reduce_fusion
  1.4 0.8 fusion.71
  2.2 2.1 %fusion.6 = f32[14,192]{1,0:T(8,128)S(1)} fusion(f32[14,64,128]{2,1,0:T(8,128)} %bitcast.119, f32[64,192]{1,0:T(8,128)S(1)} %select_add_fusion.3, f32[192]{0:T(256)S(1)} %bitcast.153, s32[192]{0:T(256)S(1)} %get-tuple-element.50, f32[192]{0:T(256)S(1)} %broadcast_subtract_fusion.1, s32[192]{0:T(256)S(1)} %get-tuple-element.49), kind=kOutput, calls=%fused_computation.9 | convolution fusion | flops 264705408 | bytes 521728 | tf_op jit(solution)/shard_map/kij,sj->kis/dot_general | solution.py:113
  4.5 23.7 %all-gather = f32[16,192,14]{1,2,0:T(8,128)S(1)} all-gather(f32[1,192,14]{1,2,0:T(8,128)S(1)} %bitcast.145), channel_id=1, replica_groups=mesh['panel'=2,'lat'=4,'lon'=4] {'lat','lon'}, dimensions={0}, use_global_device_ids=true | all-gather | bytes 182784 | tf_op jit(solution)/shard_map/all_gather | solution.py:118
  28.4 1.3 %collective-permute-start = (f32[14,3072]{1,0:T(8,128)S(1)}, f32[14,3072]{1,0:T(8,128)S(1)}, u32[]{:S(2)}, u32[]{:S(2)}) collective-permute-start(f32[14,3072]{1,0:T(8,128)S(1)} %bitcast.127), channel_id=1, source_target_pairs={{0,16},{16,0},{1,17},{17,1},{2,18},{18,2},{3,19},{19,3},{4,20},{20... | collective-permute-start | bytes 516104 | tf_op jit(solution)/shard_map/ppermute | solution.py:21
  29.9 2.4 %collective-permute-start.3 = (f32[7,2,64,2]{3,2,1,0:T(8,128)S(1)}, f32[7,2,64,2]{3,2,1,0:T(8,128)S(1)}, u32[]{:S(2)}, u32[]{:S(2)}) collective-permute-start(f32[7,2,64,2]{3,2,1,0:T(8,128)S(1)} %get-tuple-element.36), channel_id=1, source_target_pairs={{1,0},{2,1},{3,2},{5,4},{6,5},{7,6},{9,8},{10,9},{11,10},{13,12},{... | collective-permute-start | bytes 21512 | tf_op jit(solution)/shard_map/ppermute | solution.py:30
  32.3 3.2 %collective-permute-start.4 = (f32[7,2,64,2]{3,2,1,0:T(8,128)S(1)}, f32[7,2,64,2]{3,2,1,0:T(8,128)S(1)}, u32[]{:S(2)}, u32[]{:S(2)}) collective-permute-start(f32[7,2,64,2]{3,2,1,0:T(8,128)S(1)} %get-tuple-element.35), channel_id=1, source_target_pairs={{0,1},{1,2},{2,3},{4,5},{5,6},{6,7},{8,9},{9,10},{10,11},{12,13},{... | collective-permute-start | bytes 21512 | tf_op jit(solution)/shard_map/ppermute | solution.py:30
  35.5 1.3 %collective-permute-start.1 = (f32[7,2,2,128]{3,2,1,0:T(2,128)S(1)}, f32[7,2,2,128]{3,2,1,0:T(2,128)S(1)}, u32[]{:S(2)}, u32[]{:S(2)}) collective-permute-start(f32[7,2,2,128]{3,2,1,0:T(2,128)S(1)} %get-tuple-element.38), channel_id=1, source_target_pairs={{4,0},{8,4},{12,8},{5,1},{9,5},{13,9},{6,2},{10,6},{14,10},{7,3},{... | collective-permute-start | bytes 43016 | tf_op jit(solution)/shard_map/ppermute | solution.py:30
  36.8 4.0 %collective-permute-start.2 = (f32[7,2,2,128]{3,2,1,0:T(2,128)S(1)}, f32[7,2,2,128]{3,2,1,0:T(2,128)S(1)}, u32[]{:S(2)}, u32[]{:S(2)}) collective-permute-start(f32[7,2,2,128]{3,2,1,0:T(2,128)S(1)} %get-tuple-element.37), channel_id=1, source_target_pairs={{0,4},{4,8},{8,12},{1,5},{5,9},{9,13},{2,6},{6,10},{10,14},{3,7},{... | collective-permute-start | bytes 43016 | tf_op jit(solution)/shard_map/ppermute | solution.py:30
  40.9 1.5 %fusion.1 = f32[14,384]{1,0:T(8,128)S(1)} fusion(f32[14,3072]{1,0:T(8,128)S(1)} %collective-permute-done, s32[384]{0:T(512)S(1)} %pad_add_fusion), kind=kOutput, calls=%fused_computation.2 | convolution fusion | flops 199360512 | bytes 195072 | tf_op jit(solution)/shard_map/dot_general | solution.py:120
  43.0 0.9 %multiply_add_fusion.2 = (f32[7,2,64,128]{3,2,1,0:T(8,128)S(1)}, f32[7,2,64,128]{3,2,1,0:T(8,128)S(1)}, f32[7,2,64,128]{3,2,1,0:T(8,128)S(1)}) fusion(f32[2,64,128]{2,1,0:T(8,128)S(1)} %get-tuple-element.30, f32[2,64,128]{2,1,0:T(8,128)S(1)} %get-tuple-element.31, f32[7,2,64,128]{3,2,1,0:T(8,128)S(1)} %bitcast.122, ...), kind=kLoop, calls=%fused_computation.74 | loop fusion | flops 2179072 | bytes 2009088 | tf_op jit(solution)/shard_map/add | solution.py:52
  44.7 0.9 %fusion.66 = (f32[7,2,64,2]{3,2,1,0:T(8,128)S(1)}, f32[7,2,64,2]{3,2,1,0:T(8,128)}) fusion(f32[7,2,64,128]{3,2,1,0:T(8,128)S(1)} %get-tuple-element.28), kind=kLoop, calls=%fused_computation.175 | loop fusion | bytes 28672 | tf_op jit(solution)/shard_map/slice | solution.py:125
  45.7 1.0 %fusion.5 = f32[14,192]{1,0:T(8,128)S(1)} fusion(f32[14,64,128]{2,1,0:T(8,128)S(1)} %bitcast_add_fusion, f32[64,192]{1,0:T(8,128)S(1)} %select_add_fusion.3, f32[192]{0:T(256)S(1)} %bitcast.154, s32[192]{0:T(256)S(1)} %get-tuple-element.50, f32[192]{0:T(256)S(1)} %broadcast_subtract_fusion.1, s32[192]{0:T(256)S(1)} %get-tuple-element.49), kind=kOutput, calls=%fused_computation.8 | convolution fusion | flops 264705408 | bytes 521728 | tf_op jit(solution)/shard_map/kij,sj->kis/dot_general | solution.py:113
  46.9 18.7 %all-gather.1 = f32[16,192,14]{1,2,0:T(8,128)S(1)} all-gather(f32[1,192,14]{1,2,0:T(8,128)S(1)} %bitcast.146), channel_id=1, replica_groups=mesh['panel'=2,'lat'=4,'lon'=4] {'lat','lon'}, dimensions={0}, use_global_device_ids=true | all-gather | bytes 182784 | tf_op jit(solution)/shard_map/all_gather | solution.py:118
  65.8 0.6 collective-permute-start.5
  66.5 2.3 %collective-permute-start.8 = (f32[7,2,64,2]{3,2,1,0:T(8,128)}, f32[7,2,64,2]{3,2,1,0:T(8,128)S(1)}, u32[]{:S(2)}, u32[]{:S(2)}) collective-permute-start(f32[7,2,64,2]{3,2,1,0:T(8,128)} %get-tuple-element.24), channel_id=1, source_target_pairs={{1,0},{2,1},{3,2},{5,4},{6,5},{7,6},{9,8},{10,9},{11,10},{13,12},{... | collective-permute-start | bytes 21512 | tf_op jit(solution)/shard_map/ppermute | solution.py:30
  68.8 3.2 %collective-permute-start.9 = (f32[7,2,64,2]{3,2,1,0:T(8,128)S(1)}, f32[7,2,64,2]{3,2,1,0:T(8,128)}, u32[]{:S(2)}, u32[]{:S(2)}) collective-permute-start(f32[7,2,64,2]{3,2,1,0:T(8,128)S(1)} %get-tuple-element.23), channel_id=1, source_target_pairs={{0,1},{1,2},{2,3},{4,5},{5,6},{6,7},{8,9},{9,10},{10,11},{12,13},{... | collective-permute-start | bytes 21512 | tf_op jit(solution)/shard_map/ppermute | solution.py:30
  72.1 1.3 %collective-permute-start.6 = (f32[7,2,2,128]{3,2,1,0:T(2,128)S(1)}, f32[7,2,2,128]{3,2,1,0:T(2,128)S(1)}, u32[]{:S(2)}, u32[]{:S(2)}) collective-permute-start(f32[7,2,2,128]{3,2,1,0:T(2,128)S(1)} %get-tuple-element.26), channel_id=1, source_target_pairs={{4,0},{8,4},{12,8},{5,1},{9,5},{13,9},{6,2},{10,6},{14,10},{7,3},{... | collective-permute-start | bytes 43016 | tf_op jit(solution)/shard_map/ppermute | solution.py:30
  73.4 4.6 %collective-permute-start.7 = (f32[7,2,2,128]{3,2,1,0:T(2,128)S(1)}, f32[7,2,2,128]{3,2,1,0:T(2,128)}, u32[]{:S(2)}, u32[]{:S(2)}) collective-permute-start(f32[7,2,2,128]{3,2,1,0:T(2,128)S(1)} %get-tuple-element.25), channel_id=1, source_target_pairs={{0,4},{4,8},{8,12},{1,5},{5,9},{9,13},{2,6},{6,10},{10,14},{3,7},{... | collective-permute-start | bytes 43016 | tf_op jit(solution)/shard_map/ppermute | solution.py:30
  78.0 1.5 %fusion = f32[14,384]{1,0:T(8,128)S(1)} fusion(f32[14,3072]{1,0:T(8,128)S(1)} %collective-permute-done.5, s32[384]{0:T(512)S(1)} %pad_add_fusion), kind=kOutput, calls=%fused_computation.1 | convolution fusion | flops 199360512 | bytes 195072 | tf_op jit(solution)/shard_map/dot_general | solution.py:120
  79.8 1.1 %bitcast_select_fusion = (f32[7,2,64,2]{3,2,1,0:T(8,128)S(1)}, f32[7,2,64,2]{3,2,1,0:T(8,128)S(1)}) fusion(f32[7,2,64,2]{3,2,1,0:T(8,128)} %collective-permute-done.9, f32[7,2,2,64]{2,3,1,0:T(8,128)S(1)} %copy.21, pred[]{:T(512)S(6)} %eq.104, f32[7,2,64,2]{3,2,1,0:T(8,128)S(1)} %collective-permute-done.8, pred[]{:T(512)S(6)} %eq.107), kind=kLoop, calls=%fused_computation.67 | loop fusion | flops 3584 | bytes 35842 | tf_op jit(solution)/shard_map/jit(_where)/select_n | solution.py:132
  81.6 0.9 %multiply_add_fusion = (f32[7,2,64,128]{3,2,1,0:T(8,128)S(1)}, f32[7,2,64,128]{3,2,1,0:T(8,128)S(1)}, f32[7,2,64,128]{3,2,1,0:T(8,128)S(1)}) fusion(f32[2,64,128]{2,1,0:T(8,128)S(1)} %get-tuple-element.20, f32[2,64,128]{2,1,0:T(8,128)S(1)} %get-tuple-element.18, f32[7,2,64,128]{3,2,1,0:T(8,128)S(1)} %get-tuple-element.28, ...), kind=kLoop, calls=%fused_computation.72 | loop fusion | flops 2179072 | bytes 2009088 | tf_op jit(solution)/shard_map/add | solution.py:52
  82.7 0.9 %fusion.32 = f32[1,7,2,64,128]{4,3,2,1,0:T(8,128)} fusion(f32[1,7,2,64,128]{4,3,2,1,0:T(8,128)S(1)} %copy-done, f32[1,1,2,64,128]{4,3,2,1,0:T(8,128)S(1)} %bitcast.126, f32[1,3,2,64,128]{4,3,2,1,0:T(8,128)S(1)} %bitcast.124, f32[1,2,2,64,128]{4,3,2,1,0:T(8,128)S(1)} %get-tuple-element.40, f32[1,1,2,64,128]{4,3,2,1,0:T(8,128)S(1)} %bitcast.125, ...), kind=kLoop, calls=%fused_computation.64 | loop fusion | flops 1376256 | bytes 1835008 | tf_op jit(solution)/shard_map/add | solution.py:139
  (77 shorter events, 3.6 us)
Async XLA Ops:
  0.0 4.3 %copy-start.2 = (f32[1,1,1,192]{3,2,1,0:T(1,128)S(1)}, f32[1,1,1,192]{3,2,1,0:T(1,128)}, u32[]{:S(2)}) copy-start(f32[1,1,1,192]{3,2,1,0:T(1,128)} %param.9) | copy-start | bytes 2308
  28.1 1.6 %copy-start = (f32[1,7,2,64,128]{4,3,2,1,0:T(8,128)S(1)}, f32[1,7,2,64,128]{4,3,2,1,0:T(8,128)}, u32[]{:S(2)}) copy-start(f32[1,7,2,64,128]{4,3,2,1,0:T(8,128)} %param.5) | copy-start | bytes 1376260
  28.4 12.5 %collective-permute-start = (f32[14,3072]{1,0:T(8,128)S(1)}, f32[14,3072]{1,0:T(8,128)S(1)}, u32[]{:S(2)}, u32[]{:S(2)}) collective-permute-start(f32[14,3072]{1,0:T(8,128)S(1)} %bitcast.127), channel_id=1, source_target_pairs={{0,16},{16,0},{1,17},{17,1},{2,18},{18,2},{3,19},{19,3},{4,20},{20... | collective-permute-start | bytes 516104 | tf_op jit(solution)/shard_map/ppermute | solution.py:21
  29.9 11.0 %copy-start.1 = (s32[1,1,1,768]{3,2,1,0:T(1,128)S(1)}, s32[1,1,1,768]{3,2,1,0:T(1,128)}, u32[]{:S(2)}) copy-start(s32[1,1,1,768]{3,2,1,0:T(1,128)} %param.6) | copy-start | bytes 9220
  29.9 12.9 %collective-permute-start.3 = (f32[7,2,64,2]{3,2,1,0:T(8,128)S(1)}, f32[7,2,64,2]{3,2,1,0:T(8,128)S(1)}, u32[]{:S(2)}, u32[]{:S(2)}) collective-permute-start(f32[7,2,64,2]{3,2,1,0:T(8,128)S(1)} %get-tuple-element.36), channel_id=1, source_target_pairs={{1,0},{2,1},{3,2},{5,4},{6,5},{7,6},{9,8},{10,9},{11,10},{13,12},{... | collective-permute-start | bytes 21512 | tf_op jit(solution)/shard_map/ppermute | solution.py:30
  32.3 10.5 %collective-permute-start.4 = (f32[7,2,64,2]{3,2,1,0:T(8,128)S(1)}, f32[7,2,64,2]{3,2,1,0:T(8,128)S(1)}, u32[]{:S(2)}, u32[]{:S(2)}) collective-permute-start(f32[7,2,64,2]{3,2,1,0:T(8,128)S(1)} %get-tuple-element.35), channel_id=1, source_target_pairs={{0,1},{1,2},{2,3},{4,5},{5,6},{6,7},{8,9},{9,10},{10,11},{12,13},{... | collective-permute-start | bytes 21512 | tf_op jit(solution)/shard_map/ppermute | solution.py:30
  35.5 7.5 %collective-permute-start.1 = (f32[7,2,2,128]{3,2,1,0:T(2,128)S(1)}, f32[7,2,2,128]{3,2,1,0:T(2,128)S(1)}, u32[]{:S(2)}, u32[]{:S(2)}) collective-permute-start(f32[7,2,2,128]{3,2,1,0:T(2,128)S(1)} %get-tuple-element.38), channel_id=1, source_target_pairs={{4,0},{8,4},{12,8},{5,1},{9,5},{13,9},{6,2},{10,6},{14,10},{7,3},{... | collective-permute-start | bytes 43016 | tf_op jit(solution)/shard_map/ppermute | solution.py:30
  36.8 6.2 %collective-permute-start.2 = (f32[7,2,2,128]{3,2,1,0:T(2,128)S(1)}, f32[7,2,2,128]{3,2,1,0:T(2,128)S(1)}, u32[]{:S(2)}, u32[]{:S(2)}) collective-permute-start(f32[7,2,2,128]{3,2,1,0:T(2,128)S(1)} %get-tuple-element.37), channel_id=1, source_target_pairs={{0,4},{4,8},{8,12},{1,5},{5,9},{9,13},{2,6},{6,10},{10,14},{3,7},{... | collective-permute-start | bytes 43016 | tf_op jit(solution)/shard_map/ppermute | solution.py:30
  65.8 12.1 %collective-permute-start.5 = (f32[14,3072]{1,0:T(8,128)S(1)}, f32[14,3072]{1,0:T(8,128)S(1)}, u32[]{:S(2)}, u32[]{:S(2)}) collective-permute-start(f32[14,3072]{1,0:T(8,128)S(1)} %bitcast.128), channel_id=1, source_target_pairs={{0,16},{16,0},{1,17},{17,1},{2,18},{18,2},{3,19},{19,3},{4,20},{20... | collective-permute-start | bytes 516104 | tf_op jit(solution)/shard_map/ppermute | solution.py:21
  66.5 13.3 %collective-permute-start.8 = (f32[7,2,64,2]{3,2,1,0:T(8,128)}, f32[7,2,64,2]{3,2,1,0:T(8,128)S(1)}, u32[]{:S(2)}, u32[]{:S(2)}) collective-permute-start(f32[7,2,64,2]{3,2,1,0:T(8,128)} %get-tuple-element.24), channel_id=1, source_target_pairs={{1,0},{2,1},{3,2},{5,4},{6,5},{7,6},{9,8},{10,9},{11,10},{13,12},{... | collective-permute-start | bytes 21512 | tf_op jit(solution)/shard_map/ppermute | solution.py:30
  68.8 11.0 %collective-permute-start.9 = (f32[7,2,64,2]{3,2,1,0:T(8,128)S(1)}, f32[7,2,64,2]{3,2,1,0:T(8,128)}, u32[]{:S(2)}, u32[]{:S(2)}) collective-permute-start(f32[7,2,64,2]{3,2,1,0:T(8,128)S(1)} %get-tuple-element.23), channel_id=1, source_target_pairs={{0,1},{1,2},{2,3},{4,5},{5,6},{6,7},{8,9},{9,10},{10,11},{12,13},{... | collective-permute-start | bytes 21512 | tf_op jit(solution)/shard_map/ppermute | solution.py:30
  72.1 9.0 %collective-permute-start.6 = (f32[7,2,2,128]{3,2,1,0:T(2,128)S(1)}, f32[7,2,2,128]{3,2,1,0:T(2,128)S(1)}, u32[]{:S(2)}, u32[]{:S(2)}) collective-permute-start(f32[7,2,2,128]{3,2,1,0:T(2,128)S(1)} %get-tuple-element.26), channel_id=1, source_target_pairs={{4,0},{8,4},{12,8},{5,1},{9,5},{13,9},{6,2},{10,6},{14,10},{7,3},{... | collective-permute-start | bytes 43016 | tf_op jit(solution)/shard_map/ppermute | solution.py:30
  73.4 7.7 %collective-permute-start.7 = (f32[7,2,2,128]{3,2,1,0:T(2,128)S(1)}, f32[7,2,2,128]{3,2,1,0:T(2,128)}, u32[]{:S(2)}, u32[]{:S(2)}) collective-permute-start(f32[7,2,2,128]{3,2,1,0:T(2,128)S(1)} %get-tuple-element.25), channel_id=1, source_target_pairs={{0,4},{4,8},{8,12},{1,5},{5,9},{9,13},{2,6},{6,10},{10,14},{3,7},{... | collective-permute-start | bytes 43016 | tf_op jit(solution)/shard_map/ppermute | solution.py:30
where the time goes:
time: 84.2 us; the launch traced here: 83.6 us
  blocking collectives  42.4 us (50%)
  starting transfers between devices  24.2 us (29%)
  other arithmetic  7.14 us (8%)
  matrix products  6.06 us (7%)
  local copies, waits for them, and re-layouts  3.29 us (4%)
    all_gather x2, blocking collectives, receive(): whole = lax.all_gather(given, ('lat', 'lon'), axis=1, tiled=True)  42.4 us
    ppermute x8, starting transfers between devices, shift(): return lax.ppermute(value, axis, route)  22.3 us
    dot_general x2, matrix products, donate(): along = jnp.einsum('kij,sj->kis', flat, weight_lon, precision=HIGHEST)  3.09 us
    dot_general x2, matrix products, receive(): return jnp.dot(partner, pick, precision=HIGHEST)  2.97 us
    ppermute x2, starting transfers between devices, partner_2(): return lax.ppermute(block, axis, route)  1.94 us
    add x2, other arithmetic, rate(): adv_b = middle[4:5] * d_lat + middle[5:6] * d_lon  1.8 us
  transfers between devices with their start and end apart: 10, of which 0 were waited for; matrix products, arithmetic and copies ran while one was open for 6% of the time, Pallas kernels for 0%

commit v1 on v0

--- a/solution.py
+++ b/solution.py
@@ -9,6 +9,27 @@
 buoyancy = 0.5
 time_step = 0.25
 HIGHEST = lax.Precision.HIGHEST
+
+
+def joined_along(blocks, dim):
+    shape = list(blocks.shape[1:])
+    shape[dim] *= blocks.shape[0]
+    return jnp.moveaxis(blocks, 0, dim).reshape(shape)
+
+
+def grow_blocks(x, axis):
+    peers, index = (lax.axis_size(axis), lax.axis_index(axis))
+    blocks, stride = (x[None], 1)
+    while stride < peers:
+        other = lax.ppermute(blocks, axis, [(i, i ^ stride) for i in range(peers)])
+        low = index & stride == 0
+        blocks = jnp.concatenate([jnp.where(low, blocks, other), jnp.where(low, other, blocks)])
+        stride *= 2
+    return blocks
+
+
+def doubled_up(x, axis, dim):
+    return joined_along(grow_blocks(x, axis), dim)
 
 
 def partner_2(block, axis, apart):
@@ -115,7 +136,7 @@
         return rotate(value.reshape(comps, levels, -1), turn).reshape(comps * levels, -1)
 
     def receive(given):
-        whole = lax.all_gather(given, ("lat", "lon"), axis=1, tiled=True)
+        whole = doubled_up(given, ("lat", "lon"), 1)
         partner = partner_2(whole, "panel", 0)
         return jnp.dot(partner, pick, precision=HIGHEST)
 

time: 84.2 us -> 80.7 us (0.958)
  the two profiles are of different devices: /device:TPU:1 before, /device:TPU:0 now
where the time goes in v1:
time: 80.7 us; the launch traced here: 80.2 us
  starting transfers between devices  38.1 us (47%)
  waiting for transfers between devices  23.3 us (29%)
  other arithmetic  7.41 us (9%)
  matrix products  6.05 us (7%)
  local copies, waits for them, and re-layouts  4.58 us (6%)
    ppermute x8, starting transfers between devices, shift(): return lax.ppermute(value, axis, route)  22.3 us
    ppermute x8, waiting for transfers between devices, grow_blocks(): other = lax.ppermute(blocks, axis, [(i, i ^ stride) for i in range(peers)])  15 us
    ppermute x8, starting transfers between devices, grow_blocks(): other = lax.ppermute(blocks, axis, [(i, i ^ stride) for i in range(peers)])  12.6 us
    ppermute x2, waiting for transfers between devices, partner_2(): return lax.ppermute(block, axis, route)  8.35 us
    ppermute x2, starting transfers between devices, partner_2(): return lax.ppermute(block, axis, route)  3.17 us
    dot_general x2, matrix products, donate(): along = jnp.einsum('kij,sj->kis', flat, weight_lon, precision=HIGHEST)  3.08 us
    dot_general x2, matrix products, receive(): return jnp.dot(partner, pick, precision=HIGHEST)  2.97 us
    add x2, other arithmetic, rate(): adv_b = middle[4:5] * d_lat + middle[5:6] * d_lon  1.8 us
  transfers between devices with their start and end apart: 18, of which 7 were waited for; matrix products, arithmetic and copies ran while one was open for 8% of the time, Pallas kernels for 0%

profile of v1, /device:TPU:0, one launch (start us, length us, event | category | flops | bytes accessed | tf_op | source)
XLA Modules:
  0.0 80.2 jit_solution(12013276738112275311)
XLA Ops:
  2.8 2.1 %fusion.6 = f32[14,192]{1,0:T(8,128)S(1)} fusion(f32[14,64,128]{2,1,0:T(8,128)} %bitcast.111, f32[64,192]{1,0:T(8,128)S(1)} %select_add_fusion.3, f32[192]{0:T(256)S(1)} %bitcast.141, s32[192]{0:T(256)S(1)} %get-tuple-element.66, f32[192]{0:T(256)S(1)} %broadcast_subtract_fusion.1, s32[192]{0:T(256)S(1)} %get-tuple-element.65), kind=kOutput, calls=%fused_computation.9 | convolution fusion | flops 264705408 | bytes 521728 | tf_op jit(solution)/shard_map/kij,sj->kis/dot_general | solution.py:134
  5.8 1.3 %collective-permute-start.7 = (f32[7,2,64,2]{3,2,1,0:T(8,128)S(1)}, f32[7,2,64,2]{3,2,1,0:T(8,128)S(1)}, u32[]{:S(2)}, u32[]{:S(2)}) collective-permute-start(f32[7,2,64,2]{3,2,1,0:T(8,128)S(1)} %get-tuple-element.36), channel_id=1, source_target_pairs={{1,0},{2,1},{3,2},{5,4},{6,5},{7,6},{9,8},{10,9},{11,10},{13,12},{... | collective-permute-start | bytes 21512 | tf_op jit(solution)/shard_map/ppermute | solution.py:51
  7.1 3.1 %collective-permute-start.8 = (f32[7,2,64,2]{3,2,1,0:T(8,128)S(1)}, f32[7,2,64,2]{3,2,1,0:T(8,128)S(1)}, u32[]{:S(2)}, u32[]{:S(2)}) collective-permute-start(f32[7,2,64,2]{3,2,1,0:T(8,128)S(1)} %get-tuple-element.35), channel_id=1, source_target_pairs={{0,1},{1,2},{2,3},{4,5},{5,6},{6,7},{8,9},{9,10},{10,11},{12,13},{... | collective-permute-start | bytes 21512 | tf_op jit(solution)/shard_map/ppermute | solution.py:51
  10.2 2.6 %collective-permute-start.1 = (f32[2,14,192]{2,1,0:T(8,128)S(1)}, f32[2,14,192]{2,1,0:T(8,128)S(1)}, u32[]{:S(2)}, u32[]{:S(2)}) collective-permute-start(f32[2,14,192]{2,1,0:T(8,128)S(1)} %pad_maximum_fusion.12), channel_id=1, source_target_pairs={{0,2},{1,3},{2,0},{3,1},{4,6},{5,7},{6,4},{7,5},{8,10},{9,11},{10,... | collective-permute-start | bytes 64520 | tf_op jit(solution)/shard_map/ppermute | solution.py:24
  12.8 1.3 %collective-permute-start.5 = (f32[7,2,2,128]{3,2,1,0:T(2,128)S(1)}, f32[7,2,2,128]{3,2,1,0:T(2,128)S(1)}, u32[]{:S(2)}, u32[]{:S(2)}) collective-permute-start(f32[7,2,2,128]{3,2,1,0:T(2,128)S(1)} %get-tuple-element.38), channel_id=1, source_target_pairs={{4,0},{8,4},{12,8},{5,1},{9,5},{13,9},{6,2},{10,6},{14,10},{7,3},{... | collective-permute-start | bytes 43016 | tf_op jit(solution)/shard_map/ppermute | solution.py:51
  14.1 5.1 %collective-permute-start.6 = (f32[7,2,2,128]{3,2,1,0:T(2,128)S(1)}, f32[7,2,2,128]{3,2,1,0:T(2,128)}, u32[]{:S(2)}, u32[]{:S(2)}) collective-permute-start(f32[7,2,2,128]{3,2,1,0:T(2,128)S(1)} %get-tuple-element.37), channel_id=1, source_target_pairs={{0,4},{4,8},{8,12},{1,5},{5,9},{9,13},{2,6},{6,10},{10,14},{3,7},{... | collective-permute-start | bytes 43016 | tf_op jit(solution)/shard_map/ppermute | solution.py:51
  19.3 1.2 %collective-permute-start.2 = (f32[4,14,192]{2,1,0:T(8,128)S(1)}, f32[4,14,192]{2,1,0:T(8,128)S(1)}, u32[]{:S(2)}, u32[]{:S(2)}) collective-permute-start(f32[4,14,192]{2,1,0:T(8,128)S(1)} %pad_maximum_fusion.10), channel_id=1, source_target_pairs={{0,4},{1,5},{2,6},{3,7},{4,0},{5,1},{6,2},{7,3},{8,12},{9,13},{10,... | collective-permute-start | bytes 129032 | tf_op jit(solution)/shard_map/ppermute | solution.py:24
  20.5 3.1 %collective-permute-done.2 = f32[4,14,192]{2,1,0:T(8,128)S(1)} collective-permute-done((f32[4,14,192]{2,1,0:T(8,128)S(1)}, f32[4,14,192]{2,1,0:T(8,128)S(1)}, u32[]{:S(2)}, u32[]{:S(2)}) %collective-permute-start.2) | collective-permute-done | bytes 43040 | tf_op jit(solution)/shard_map/ppermute | solution.py:24
  23.7 2.2 %collective-permute-start.3 = (f32[8,14,192]{2,1,0:T(8,128)S(1)}, f32[8,14,192]{2,1,0:T(8,128)S(1)}, u32[]{:S(2)}, u32[]{:S(2)}) collective-permute-start(f32[8,14,192]{2,1,0:T(8,128)S(1)} %pad_maximum_fusion.8), channel_id=1, source_target_pairs={{0,8},{1,9},{2,10},{3,11},{4,12},{5,13},{6,14},{7,15},{8,0},{9,1},... | collective-permute-start | bytes 258056 | tf_op jit(solution)/shard_map/ppermute | solution.py:24
  25.9 6.1 %collective-permute-done.3 = f32[8,14,192]{2,1,0:T(8,128)S(1)} collective-permute-done((f32[8,14,192]{2,1,0:T(8,128)S(1)}, f32[8,14,192]{2,1,0:T(8,128)S(1)}, u32[]{:S(2)}, u32[]{:S(2)}) %collective-permute-start.3) | collective-permute-done | bytes 86048 | tf_op jit(solution)/shard_map/ppermute | solution.py:24
  32.2 1.6 %collective-permute-start.4 = (f32[14,3072]{1,0:T(8,128)S(1)}, f32[14,3072]{1,0:T(8,128)S(1)}, u32[]{:S(2)}, u32[]{:S(2)}) collective-permute-start(f32[14,3072]{1,0:T(8,128)S(1)} %reshape.355), channel_id=1, source_target_pairs={{0,16},{16,0},{1,17},{17,1},{2,18},{18,2},{3,19},{19,3},{4,20},{20... | collective-permute-start | bytes 516104 | tf_op jit(solution)/shard_map/ppermute | solution.py:42
  33.9 4.1 %collective-permute-done.4 = f32[14,3072]{1,0:T(8,128)S(1)} collective-permute-done((f32[14,3072]{1,0:T(8,128)S(1)}, f32[14,3072]{1,0:T(8,128)S(1)}, u32[]{:S(2)}, u32[]{:S(2)}) %collective-permute-start.4) | collective-permute-done | bytes 172064 | tf_op jit(solution)/shard_map/ppermute | solution.py:42
  38.0 1.5 %fusion.1 = f32[14,384]{1,0:T(8,128)S(1)} fusion(f32[14,3072]{1,0:T(8,128)S(1)} %collective-permute-done.4, s32[384]{0:T(512)S(1)} %pad_add_fusion), kind=kOutput, calls=%fused_computation.2 | convolution fusion | flops 199360512 | bytes 195072 | tf_op jit(solution)/shard_map/dot_general | solution.py:141
  45.1 3.3 %collective-permute-start.10 = (f32[2,14,192]{2,1,0:T(8,128)S(1)}, f32[2,14,192]{2,1,0:T(8,128)S(1)}, u32[]{:S(2)}, u32[]{:S(2)}) collective-permute-start(f32[2,14,192]{2,1,0:T(8,128)S(1)} %pad_maximum_fusion.13), channel_id=1, source_target_pairs={{0,2},{1,3},{2,0},{3,1},{4,6},{5,7},{6,4},{7,5},{8,10},{9,11},{10,... | collective-permute-start | bytes 64520 | tf_op jit(solution)/shard_map/ppermute | solution.py:24
  48.4 1.9 %collective-permute-done.10 = f32[2,14,192]{2,1,0:T(8,128)S(1)} collective-permute-done((f32[2,14,192]{2,1,0:T(8,128)S(1)}, f32[2,14,192]{2,1,0:T(8,128)S(1)}, u32[]{:S(2)}, u32[]{:S(2)}) %collective-permute-start.10) | collective-permute-done | bytes 21536 | tf_op jit(solution)/shard_map/ppermute | solution.py:24
  51.9 2.7 %collective-permute-done.11 = f32[4,14,192]{2,1,0:T(8,128)S(1)} collective-permute-done((f32[4,14,192]{2,1,0:T(8,128)S(1)}, f32[4,14,192]{2,1,0:T(8,128)S(1)}, u32[]{:S(2)}, u32[]{:S(2)}) %collective-permute-start.11) | collective-permute-done | bytes 43040 | tf_op jit(solution)/shard_map/ppermute | solution.py:24
  54.7 2.1 %collective-permute-start.12 = (f32[8,14,192]{2,1,0:T(8,128)S(1)}, f32[8,14,192]{2,1,0:T(8,128)S(1)}, u32[]{:S(2)}, u32[]{:S(2)}) collective-permute-start(f32[8,14,192]{2,1,0:T(8,128)S(1)} %pad_maximum_fusion.9), channel_id=1, source_target_pairs={{0,8},{1,9},{2,10},{3,11},{4,12},{5,13},{6,14},{7,15},{8,0},{9,1},... | collective-permute-start | bytes 258056 | tf_op jit(solution)/shard_map/ppermute | solution.py:24
  56.8 1.3 %collective-permute-start.16 = (f32[7,2,64,2]{3,2,1,0:T(8,128)}, f32[7,2,64,2]{3,2,1,0:T(8,128)}, u32[]{:S(2)}, u32[]{:S(2)}) collective-permute-start(f32[7,2,64,2]{3,2,1,0:T(8,128)} %get-tuple-element.24), channel_id=1, source_target_pairs={{1,0},{2,1},{3,2},{5,4},{6,5},{7,6},{9,8},{10,9},{11,10},{13,12},{... | collective-permute-start | bytes 21512 | tf_op jit(solution)/shard_map/ppermute | solution.py:51
  58.0 3.8 %collective-permute-start.17 = (f32[7,2,64,2]{3,2,1,0:T(8,128)S(1)}, f32[7,2,64,2]{3,2,1,0:T(8,128)}, u32[]{:S(2)}, u32[]{:S(2)}) collective-permute-start(f32[7,2,64,2]{3,2,1,0:T(8,128)S(1)} %get-tuple-element.23), channel_id=1, source_target_pairs={{0,1},{1,2},{2,3},{4,5},{5,6},{6,7},{8,9},{9,10},{10,11},{12,13},{... | collective-permute-start | bytes 21512 | tf_op jit(solution)/shard_map/ppermute | solution.py:51
  61.9 1.3 %collective-permute-start.14 = (f32[7,2,2,128]{3,2,1,0:T(2,128)S(1)}, f32[7,2,2,128]{3,2,1,0:T(2,128)S(1)}, u32[]{:S(2)}, u32[]{:S(2)}) collective-permute-start(f32[7,2,2,128]{3,2,1,0:T(2,128)S(1)} %get-tuple-element.26), channel_id=1, source_target_pairs={{4,0},{8,4},{12,8},{5,1},{9,5},{13,9},{6,2},{10,6},{14,10},{7,3},{... | collective-permute-start | bytes 43016 | tf_op jit(solution)/shard_map/ppermute | solution.py:51
  63.2 5.2 %collective-permute-start.15 = (f32[7,2,2,128]{3,2,1,0:T(2,128)S(1)}, f32[7,2,2,128]{3,2,1,0:T(2,128)}, u32[]{:S(2)}, u32[]{:S(2)}) collective-permute-start(f32[7,2,2,128]{3,2,1,0:T(2,128)S(1)} %get-tuple-element.25), channel_id=1, source_target_pairs={{0,4},{4,8},{8,12},{1,5},{5,9},{9,13},{2,6},{6,10},{10,14},{3,7},{... | collective-permute-start | bytes 43016 | tf_op jit(solution)/shard_map/ppermute | solution.py:51
  68.7 1.6 %collective-permute-start.13 = (f32[14,3072]{1,0:T(8,128)S(1)}, f32[14,3072]{1,0:T(8,128)S(1)}, u32[]{:S(2)}, u32[]{:S(2)}) collective-permute-start(f32[14,3072]{1,0:T(8,128)S(1)} %reshape.359), channel_id=1, source_target_pairs={{0,16},{16,0},{1,17},{17,1},{2,18},{18,2},{3,19},{19,3},{4,20},{20... | collective-permute-start | bytes 516104 | tf_op jit(solution)/shard_map/ppermute | solution.py:42
  70.3 4.2 %collective-permute-done.13 = f32[14,3072]{1,0:T(8,128)S(1)} collective-permute-done((f32[14,3072]{1,0:T(8,128)S(1)}, f32[14,3072]{1,0:T(8,128)S(1)}, u32[]{:S(2)}, u32[]{:S(2)}) %collective-permute-start.13) | collective-permute-done | bytes 172064 | tf_op jit(solution)/shard_map/ppermute | solution.py:42
  74.5 1.5 %fusion = f32[14,384]{1,0:T(8,128)S(1)} fusion(f32[14,3072]{1,0:T(8,128)S(1)} %collective-permute-done.13, s32[384]{0:T(512)S(1)} %copy-done.7), kind=kOutput, calls=%fused_computation.1 | convolution fusion | flops 199360512 | bytes 195072 | tf_op jit(solution)/shard_map/dot_general | solution.py:141
  (131 shorter events, 15.5 us)
Async XLA Ops:
  0.0 5.6 %copy-start = (f32[1,7,2,64,128]{4,3,2,1,0:T(8,128)S(1)}, f32[1,7,2,64,128]{4,3,2,1,0:T(8,128)}, u32[]{:S(2)}) copy-start(f32[1,7,2,64,128]{4,3,2,1,0:T(8,128)} %param.5) | copy-start | bytes 1376260
  0.0 4.9 %copy-start.8 = (f32[1,1,1,192]{3,2,1,0:T(1,128)S(1)}, f32[1,1,1,192]{3,2,1,0:T(1,128)}, u32[]{:S(2)}) copy-start(f32[1,1,1,192]{3,2,1,0:T(1,128)} %param.9) | copy-start | bytes 2308
  2.2 2.8 %copy-start.3 = (f32[1,1,1,1,192]{4,3,2,1,0:T(1,128)}, f32[1,1,1,1,192]{4,3,2,1,0:T(1,128)S(1)}, u32[]{:S(2)}) copy-start(f32[1,1,1,1,192]{4,3,2,1,0:T(1,128)S(1)} %get-tuple-element.61) | copy-start | bytes 2308
  5.1 5.1 %collective-permute-start = (f32[1,14,192]{2,1,0:T(8,128)S(1)}, f32[1,14,192]{2,1,0:T(8,128)S(1)}, u32[]{:S(2)}, u32[]{:S(2)}) collective-permute-start(f32[1,14,192]{2,1,0:T(8,128)S(1)} %broadcast_in_dim_reshape.6), channel_id=1, source_target_pairs={{0,1},{1,0},{2,3},{3,2},{4,5},{5,4},{6,7},{7,6},{8,9},{9,8},{10,11... | collective-permute-start | bytes 32264 | tf_op jit(solution)/shard_map/ppermute | solution.py:24
  5.8 34.0 %collective-permute-start.7 = (f32[7,2,64,2]{3,2,1,0:T(8,128)S(1)}, f32[7,2,64,2]{3,2,1,0:T(8,128)S(1)}, u32[]{:S(2)}, u32[]{:S(2)}) collective-permute-start(f32[7,2,64,2]{3,2,1,0:T(8,128)S(1)} %get-tuple-element.36), channel_id=1, source_target_pairs={{1,0},{2,1},{3,2},{5,4},{6,5},{7,6},{9,8},{10,9},{11,10},{13,12},{... | collective-permute-start | bytes 21512 | tf_op jit(solution)/shard_map/ppermute | solution.py:51
  7.1 32.7 %collective-permute-start.8 = (f32[7,2,64,2]{3,2,1,0:T(8,128)S(1)}, f32[7,2,64,2]{3,2,1,0:T(8,128)S(1)}, u32[]{:S(2)}, u32[]{:S(2)}) collective-permute-start(f32[7,2,64,2]{3,2,1,0:T(8,128)S(1)} %get-tuple-element.35), channel_id=1, source_target_pairs={{0,1},{1,2},{2,3},{4,5},{5,6},{6,7},{8,9},{9,10},{10,11},{12,13},{... | collective-permute-start | bytes 21512 | tf_op jit(solution)/shard_map/ppermute | solution.py:51
  10.2 9.0 %collective-permute-start.1 = (f32[2,14,192]{2,1,0:T(8,128)S(1)}, f32[2,14,192]{2,1,0:T(8,128)S(1)}, u32[]{:S(2)}, u32[]{:S(2)}) collective-permute-start(f32[2,14,192]{2,1,0:T(8,128)S(1)} %pad_maximum_fusion.12), channel_id=1, source_target_pairs={{0,2},{1,3},{2,0},{3,1},{4,6},{5,7},{6,4},{7,5},{8,10},{9,11},{10,... | collective-permute-start | bytes 64520 | tf_op jit(solution)/shard_map/ppermute | solution.py:24
  12.8 27.2 %collective-permute-start.5 = (f32[7,2,2,128]{3,2,1,0:T(2,128)S(1)}, f32[7,2,2,128]{3,2,1,0:T(2,128)S(1)}, u32[]{:S(2)}, u32[]{:S(2)}) collective-permute-start(f32[7,2,2,128]{3,2,1,0:T(2,128)S(1)} %get-tuple-element.38), channel_id=1, source_target_pairs={{4,0},{8,4},{12,8},{5,1},{9,5},{13,9},{6,2},{10,6},{14,10},{7,3},{... | collective-permute-start | bytes 43016 | tf_op jit(solution)/shard_map/ppermute | solution.py:51
  14.1 25.9 %collective-permute-start.6 = (f32[7,2,2,128]{3,2,1,0:T(2,128)S(1)}, f32[7,2,2,128]{3,2,1,0:T(2,128)}, u32[]{:S(2)}, u32[]{:S(2)}) collective-permute-start(f32[7,2,2,128]{3,2,1,0:T(2,128)S(1)} %get-tuple-element.37), channel_id=1, source_target_pairs={{0,4},{4,8},{8,12},{1,5},{5,9},{9,13},{2,6},{6,10},{10,14},{3,7},{... | collective-permute-start | bytes 43016 | tf_op jit(solution)/shard_map/ppermute | solution.py:51
  19.3 6.6 %copy-start.5 = (s32[1,1,1,768]{3,2,1,0:T(1,128)S(1)}, s32[1,1,1,768]{3,2,1,0:T(1,128)}, u32[]{:S(2)}) copy-start(s32[1,1,1,768]{3,2,1,0:T(1,128)} %param.6) | copy-start | bytes 9220
  19.3 4.3 %collective-permute-start.2 = (f32[4,14,192]{2,1,0:T(8,128)S(1)}, f32[4,14,192]{2,1,0:T(8,128)S(1)}, u32[]{:S(2)}, u32[]{:S(2)}) collective-permute-start(f32[4,14,192]{2,1,0:T(8,128)S(1)} %pad_maximum_fusion.10), channel_id=1, source_target_pairs={{0,4},{1,5},{2,6},{3,7},{4,0},{5,1},{6,2},{7,3},{8,12},{9,13},{10,... | collective-permute-start | bytes 129032 | tf_op jit(solution)/shard_map/ppermute | solution.py:24
  23.7 8.2 %collective-permute-start.3 = (f32[8,14,192]{2,1,0:T(8,128)S(1)}, f32[8,14,192]{2,1,0:T(8,128)S(1)}, u32[]{:S(2)}, u32[]{:S(2)}) collective-permute-start(f32[8,14,192]{2,1,0:T(8,128)S(1)} %pad_maximum_fusion.8), channel_id=1, source_target_pairs={{0,8},{1,9},{2,10},{3,11},{4,12},{5,13},{6,14},{7,15},{8,0},{9,1},... | collective-permute-start | bytes 258056 | tf_op jit(solution)/shard_map/ppermute | solution.py:24
  32.2 5.7 %collective-permute-start.4 = (f32[14,3072]{1,0:T(8,128)S(1)}, f32[14,3072]{1,0:T(8,128)S(1)}, u32[]{:S(2)}, u32[]{:S(2)}) collective-permute-start(f32[14,3072]{1,0:T(8,128)S(1)} %reshape.355), channel_id=1, source_target_pairs={{0,16},{16,0},{1,17},{17,1},{2,18},{18,2},{3,19},{19,3},{4,20},{20... | collective-permute-start | bytes 516104 | tf_op jit(solution)/shard_map/ppermute | solution.py:42
  33.8 4.1 %copy-start.6 = (s32[384]{0:T(512)}, s32[384]{0:T(512)S(1)}, u32[]{:S(2)}) copy-start(s32[384]{0:T(512)S(1)} %pad_add_fusion) | copy-start | bytes 4612
  43.8 1.2 %collective-permute-start.9 = (f32[1,14,192]{2,1,0:T(8,128)S(1)}, f32[1,14,192]{2,1,0:T(8,128)S(1)}, u32[]{:S(2)}, u32[]{:S(2)}) collective-permute-start(f32[1,14,192]{2,1,0:T(8,128)S(1)} %broadcast_in_dim_reshape.7), channel_id=1, source_target_pairs={{0,1},{1,0},{2,3},{3,2},{4,5},{5,4},{6,7},{7,6},{8,9},{9,8},{10,11... | collective-permute-start | bytes 32264 | tf_op jit(solution)/shard_map/ppermute | solution.py:24
  45.1 5.2 %collective-permute-start.10 = (f32[2,14,192]{2,1,0:T(8,128)S(1)}, f32[2,14,192]{2,1,0:T(8,128)S(1)}, u32[]{:S(2)}, u32[]{:S(2)}) collective-permute-start(f32[2,14,192]{2,1,0:T(8,128)S(1)} %pad_maximum_fusion.13), channel_id=1, source_target_pairs={{0,2},{1,3},{2,0},{3,1},{4,6},{5,7},{6,4},{7,5},{8,10},{9,11},{10,... | collective-permute-start | bytes 64520 | tf_op jit(solution)/shard_map/ppermute | solution.py:24
  50.3 4.3 %collective-permute-start.11 = (f32[4,14,192]{2,1,0:T(8,128)S(1)}, f32[4,14,192]{2,1,0:T(8,128)S(1)}, u32[]{:S(2)}, u32[]{:S(2)}) collective-permute-start(f32[4,14,192]{2,1,0:T(8,128)S(1)} %pad_maximum_fusion.11), channel_id=1, source_target_pairs={{0,4},{1,5},{2,6},{3,7},{4,0},{5,1},{6,2},{7,3},{8,12},{9,13},{10,... | collective-permute-start | bytes 129032 | tf_op jit(solution)/shard_map/ppermute | solution.py:24
  54.7 13.7 %collective-permute-start.12 = (f32[8,14,192]{2,1,0:T(8,128)S(1)}, f32[8,14,192]{2,1,0:T(8,128)S(1)}, u32[]{:S(2)}, u32[]{:S(2)}) collective-permute-start(f32[8,14,192]{2,1,0:T(8,128)S(1)} %pad_maximum_fusion.9), channel_id=1, source_target_pairs={{0,8},{1,9},{2,10},{3,11},{4,12},{5,13},{6,14},{7,15},{8,0},{9,1},... | collective-permute-start | bytes 258056 | tf_op jit(solution)/shard_map/ppermute | solution.py:24
  56.8 19.6 %collective-permute-start.16 = (f32[7,2,64,2]{3,2,1,0:T(8,128)}, f32[7,2,64,2]{3,2,1,0:T(8,128)}, u32[]{:S(2)}, u32[]{:S(2)}) collective-permute-start(f32[7,2,64,2]{3,2,1,0:T(8,128)} %get-tuple-element.24), channel_id=1, source_target_pairs={{1,0},{2,1},{3,2},{5,4},{6,5},{7,6},{9,8},{10,9},{11,10},{13,12},{... | collective-permute-start | bytes 21512 | tf_op jit(solution)/shard_map/ppermute | solution.py:51
  58.0 18.3 %collective-permute-start.17 = (f32[7,2,64,2]{3,2,1,0:T(8,128)S(1)}, f32[7,2,64,2]{3,2,1,0:T(8,128)}, u32[]{:S(2)}, u32[]{:S(2)}) collective-permute-start(f32[7,2,64,2]{3,2,1,0:T(8,128)S(1)} %get-tuple-element.23), channel_id=1, source_target_pairs={{0,1},{1,2},{2,3},{4,5},{5,6},{6,7},{8,9},{9,10},{10,11},{12,13},{... | collective-permute-start | bytes 21512 | tf_op jit(solution)/shard_map/ppermute | solution.py:51
  61.9 15.7 %collective-permute-start.14 = (f32[7,2,2,128]{3,2,1,0:T(2,128)S(1)}, f32[7,2,2,128]{3,2,1,0:T(2,128)S(1)}, u32[]{:S(2)}, u32[]{:S(2)}) collective-permute-start(f32[7,2,2,128]{3,2,1,0:T(2,128)S(1)} %get-tuple-element.26), channel_id=1, source_target_pairs={{4,0},{8,4},{12,8},{5,1},{9,5},{13,9},{6,2},{10,6},{14,10},{7,3},{... | collective-permute-start | bytes 43016 | tf_op jit(solution)/shard_map/ppermute | solution.py:51
  63.2 14.4 %collective-permute-start.15 = (f32[7,2,2,128]{3,2,1,0:T(2,128)S(1)}, f32[7,2,2,128]{3,2,1,0:T(2,128)}, u32[]{:S(2)}, u32[]{:S(2)}) collective-permute-start(f32[7,2,2,128]{3,2,1,0:T(2,128)S(1)} %get-tuple-element.25), channel_id=1, source_target_pairs={{0,4},{4,8},{8,12},{1,5},{5,9},{9,13},{2,6},{6,10},{10,14},{3,7},{... | collective-permute-start | bytes 43016 | tf_op jit(solution)/shard_map/ppermute | solution.py:51
  68.5 6.0 %copy-start.7 = (s32[384]{0:T(512)S(1)}, s32[384]{0:T(512)}, u32[]{:S(2)}) copy-start(s32[384]{0:T(512)} %copy-done.6) | copy-start | bytes 4612
  68.7 5.8 %collective-permute-start.13 = (f32[14,3072]{1,0:T(8,128)S(1)}, f32[14,3072]{1,0:T(8,128)S(1)}, u32[]{:S(2)}, u32[]{:S(2)}) collective-permute-start(f32[14,3072]{1,0:T(8,128)S(1)} %reshape.359), channel_id=1, source_target_pairs={{0,16},{16,0},{1,17},{17,1},{2,18},{18,2},{3,19},{19,3},{4,20},{20... | collective-permute-start | bytes 516104 | tf_op jit(solution)/shard_map/ppermute | solution.py:42
  (9 other events, 8.4 us)
